TPU v7x, 256 devices: a whole 4x4x8 slice. The times are simulated.
256 devices in a mesh: prompt: 16 (over x_hi, z), resp: 8 (over x_lo, y), head: 2 (over core).
Axes of the slice: x: 4 (x_hi: 2, x_lo: 2; x = x_hi * 2 + x_lo), y: 4, z: 8, core: 2. Of those that a mesh axis runs over, the one named last changes fastest.
Arguments:
- prompt_q: bfloat16 [8, 1024, 4, 512], P('resp', 'prompt', None, 'head'), may hold values from -250 to 250
- prompt_kv: bfloat16 [2, 8, 1024, 512], P(None, 'resp', 'prompt'), may hold values from -8 to 8
- prompt_grad: bfloat16 [8, 1024, 4, 512], P('resp', 'prompt', None, 'head'), may hold values from -6 to 6
- resp_q: bfloat16 [16, 8, 8, 64, 4, 512], P('prompt', 'resp', None, None, None, 'head'), may hold values from -250 to 250
- resp_kv: bfloat16 [2, 16, 8, 8, 64, 512], P(None, 'prompt', 'resp'), may hold values from -6 to 6
- resp_grad: bfloat16 [16, 8, 8, 64, 4, 512], P('prompt', 'resp', None, None, None, 'head'), may hold values from -6 to 6
- resp_prompt: int32 [16, 8, 8], P('prompt', 'resp'), may hold values from 0 to 7, as said below
Outputs:
- prompt_out: bfloat16 [8, 1024, 4, 512], P('resp', 'prompt', None, 'head')
- prompt_dq: bfloat16 [8, 1024, 4, 512], P('resp', 'prompt', None, 'head')
- prompt_dkv: bfloat16 [2, 8, 1024, 512], P(None, 'resp', 'prompt', 'head')
- resp_out: bfloat16 [16, 8, 8, 64, 4, 512], P('prompt', 'resp', None, None, None, 'head')
- resp_dq: bfloat16 [16, 8, 8, 64, 4, 512], P('prompt', 'resp', None, None, None, 'head')
- resp_dkv: bfloat16 [2, 16, 8, 8, 64, 512], P(None, 'prompt', 'resp', None, None, 'head')
Inputs may be any that keep to these rules, and one draw needn't show every extreme that they name: `resp_prompt`: entry [p, r, j] is the prompt of response j held at prompt index p and resp index r; each row of 8 entries names every prompt once.
All inputs are finite; a program needn't handle non-finite values.
Results may differ from a plain program's by a relative error of at most 0.0095.
Values may be sent and summed in bfloat16 or wider, within the bound.
No kernel may reach another device: no remote copies, remote signals or barrier semaphores. Data moves between devices by JAX's collectives and lax.ppermute only.
A program may use at most 128 MiB of HBM per device.

v0:
```python
import math
import jax
import jax.numpy as jnp
from jax import lax
from jax.sharding import PartitionSpec as P

HD = 128


def attend_blocks(queries, keys_in, values_in, own_keys, own_values, cotangent, shared_ok, own_ok):
    scale = 1.0 / math.sqrt(HD)
    f32 = jnp.float32
    s_sh = jnp.einsum("brkgd,nkd->bkgrn", queries, keys_in, preferred_element_type=f32) * scale
    s_own = jnp.einsum("brkgd,bukd->bkgru", queries, own_keys, preferred_element_type=f32) * scale
    s_sh = jnp.where(shared_ok[:, None, None], s_sh, -1e30)
    s_own = jnp.where(own_ok[:, None, None], s_own, -1e30)
    row_max = jnp.maximum(
        jnp.max(s_sh, axis=-1, keepdims=True), jnp.max(s_own, axis=-1, keepdims=True)
    )
    totals = jnp.sum(jnp.exp(s_sh - row_max), axis=-1, keepdims=True) + jnp.sum(
        jnp.exp(s_own - row_max), axis=-1, keepdims=True
    )
    log_total = row_max + jnp.log(totals)
    p_sh = jnp.exp(s_sh - log_total)
    p_own = jnp.exp(s_own - log_total)
    w_sh = p_sh.astype(jnp.bfloat16)
    w_own = p_own.astype(jnp.bfloat16)
    output = (
        jnp.einsum("bkgrn,nkd->brkgd", w_sh, values_in, preferred_element_type=f32)
        + jnp.einsum("bkgru,bukd->brkgd", w_own, own_values, preferred_element_type=f32)
    ).astype(jnp.bfloat16)
    row_delta = jnp.einsum("brkgd,brkgd->bkgr", cotangent, output, preferred_element_type=f32)
    dp_sh = jnp.einsum("brkgd,nkd->bkgrn", cotangent, values_in, preferred_element_type=f32)
    dp_own = jnp.einsum("brkgd,bukd->bkgru", cotangent, own_values, preferred_element_type=f32)
    ds_sh = (p_sh * (dp_sh - row_delta[..., None])).astype(jnp.bfloat16)
    ds_own = (p_own * (dp_own - row_delta[..., None])).astype(jnp.bfloat16)
    dquery = (
        jnp.einsum("bkgrn,nkd->brkgd", ds_sh, keys_in, preferred_element_type=f32)
        + jnp.einsum("bkgru,bukd->brkgd", ds_own, own_keys, preferred_element_type=f32)
    ) * scale
    dk_sh = jnp.einsum("bkgrn,brkgd->nkd", ds_sh, queries, preferred_element_type=f32) * scale
    dv_sh = jnp.einsum("bkgrn,brkgd->nkd", w_sh, cotangent, preferred_element_type=f32)
    dk_own = jnp.einsum("bkgru,brkgd->bukd", ds_own, queries, preferred_element_type=f32) * scale
    dv_own = jnp.einsum("bkgru,brkgd->bukd", w_own, cotangent, preferred_element_type=f32)
    return (output, dquery, dk_sh, dv_sh, dk_own, dv_own)


def body(prompt_q, prompt_kv, prompt_grad, resp_q, resp_kv, resp_grad, resp_prompt):
    head_size = HD
    block_rows = prompt_q.shape[1]
    kv_heads = prompt_q.shape[2]
    local_width = prompt_q.shape[3]
    local_heads = local_width // head_size
    full_len = block_rows * lax.axis_size("prompt")
    resp_len = resp_q.shape[3]
    peers = lax.axis_size("resp")
    kv_width = kv_heads * head_size
    gathered = lax.all_gather(prompt_kv, "prompt", axis=2, tiled=True)
    prompt_keys = gathered[0, 0].reshape(full_len, kv_heads, head_size)
    prompt_values = gathered[1, 0].reshape(full_len, kv_heads, head_size)
    order = resp_prompt[0, 0]
    picker = (jnp.arange(peers)[:, None] == order[None, :]).astype(jnp.bfloat16)
    send_q = jnp.einsum(
        "dj,jrkh->drkh", picker, resp_q[0, 0], preferred_element_type=jnp.float32
    ).astype(jnp.bfloat16)
    send_kv = jnp.einsum(
        "dj,cjrh->dcrh", picker, resp_kv[:, 0, 0], preferred_element_type=jnp.float32
    ).astype(jnp.bfloat16)
    send_grad = jnp.einsum(
        "dj,jrkh->drkh", picker, resp_grad[0, 0], preferred_element_type=jnp.float32
    ).astype(jnp.bfloat16)
    got_q, got_kv, got_grad = (
        lax.all_to_all(send_q, "resp", split_axis=0, concat_axis=0, tiled=True),
        lax.all_to_all(send_kv, "resp", split_axis=0, concat_axis=0, tiled=True),
        lax.all_to_all(send_grad, "resp", split_axis=0, concat_axis=0, tiled=True),
    )
    q_shape = (peers + 1, resp_len, kv_heads, local_heads, head_size)
    queries = jnp.concatenate([got_q, prompt_q], axis=0).reshape(q_shape)
    cotangent = jnp.concatenate([got_grad, prompt_grad], axis=0).reshape(q_shape)
    own_kv = jnp.concatenate(
        [got_kv, jnp.zeros((1,) + got_kv.shape[1:], got_kv.dtype)], axis=0
    ).reshape(peers + 1, 2, resp_len, kv_heads, head_size)
    query_rows = lax.axis_index("prompt") * block_rows + jnp.arange(block_rows)
    key_cols = jnp.arange(full_len)
    causal = key_cols[None, :] <= query_rows[:, None]
    shared_ok = jnp.concatenate([jnp.ones((peers, resp_len, full_len), bool), causal[None]], axis=0)
    steps_own = jnp.arange(resp_len)
    own_causal = steps_own[None, :] <= steps_own[:, None]
    own_ok = jnp.concatenate(
        [
            jnp.broadcast_to(own_causal, (peers, resp_len, resp_len)),
            jnp.zeros((1, resp_len, resp_len), bool),
        ],
        axis=0,
    )
    out, dq, dk_sh, dv_sh, dk_own, dv_own = attend_blocks(
        queries,
        prompt_keys,
        prompt_values,
        own_kv[:, 0],
        own_kv[:, 1],
        cotangent,
        shared_ok,
        own_ok,
    )
    out = out.reshape(peers + 1, resp_len, kv_heads, local_width)
    dq = dq.astype(jnp.bfloat16).reshape(peers + 1, resp_len, kv_heads, local_width)
    prompt_part = jnp.stack([dk_sh, dv_sh]).reshape(2, full_len, kv_width)
    head_sum = lax.psum_scatter(prompt_part, "head", scatter_dimension=2, tiled=True)
    block_sum = lax.psum_scatter(head_sum, "prompt", scatter_dimension=1, tiled=True)
    own_part = jnp.stack([dk_own[:peers], dv_own[:peers]], axis=1).reshape(
        peers, 2, resp_len, kv_width
    )
    own_sum = lax.psum_scatter(own_part, "head", scatter_dimension=3, tiled=True)
    prompt_dkv = block_sum.astype(jnp.bfloat16)[:, None]
    back_kv = own_sum.astype(jnp.bfloat16)
    ret_out, ret_dq, ret_kv = (
        lax.all_to_all(out[:peers], "resp", split_axis=0, concat_axis=0, tiled=True),
        lax.all_to_all(dq[:peers], "resp", split_axis=0, concat_axis=0, tiled=True),
        lax.all_to_all(back_kv, "resp", split_axis=0, concat_axis=0, tiled=True),
    )
    resp_out = jnp.einsum(
        "dj,drkh->jrkh", picker, ret_out, preferred_element_type=jnp.float32
    ).astype(jnp.bfloat16)[None, None]
    resp_dq = jnp.einsum(
        "dj,drkh->jrkh", picker, ret_dq, preferred_element_type=jnp.float32
    ).astype(jnp.bfloat16)[None, None]
    resp_dkv = jnp.einsum(
        "dj,dcrh->cjrh", picker, ret_kv, preferred_element_type=jnp.float32
    ).astype(jnp.bfloat16)[:, None, None]
    prompt_out = out[peers:]
    prompt_dq = dq[peers:]
    return (prompt_out, prompt_dq, prompt_dkv, resp_out, resp_dq, resp_dkv)


def solution(mesh):
    return jax.shard_map(
        body,
        mesh=mesh,
        in_specs=(
            P("resp", "prompt", None, "head"),
            P(None, "resp", "prompt", None),
            P("resp", "prompt", None, "head"),
            P("prompt", "resp", None, None, None, "head"),
            P(None, "prompt", "resp", None, None, None),
            P("prompt", "resp", None, None, None, "head"),
            P("prompt", "resp", None),
        ),
        out_specs=(
            P("resp", "prompt", None, "head"),
            P("resp", "prompt", None, "head"),
            P(None, "resp", "prompt", "head"),
            P("prompt", "resp", None, None, None, "head"),
            P("prompt", "resp", None, None, None, "head"),
            P(None, "prompt", "resp", None, None, "head"),
        ),
        check_vma=False,
    )
```

profile of v0, /device:TPU:8, one launch (start us, length us, event | category | flops | bytes accessed | tf_op | source)
XLA Modules:
  0.0 434.3 jit_solution(9284214201687019022)
XLA Ops:
  11.9 5.8 %all-to-all-start = ((bf16[8,64,4,256]{3,2,1,0:T(4,128)(2,1)}), bf16[8,64,4,256]{3,2,1,0:T(4,128)(2,1)S(1)}, u32[]{:S(2)}, u32[]{:S(2)}) async-start(bf16[8,64,4,256]{3,2,1,0:T(4,128)(2,1)} %copy.205), calls=%async_computation | async-start | bytes 2097152 | tf_op jit(solution)/shard_map/all_to_all | solution.py:73
  19.8 12.4 %all-to-all-done = bf16[8,64,4,256]{3,2,1,0:T(4,128)(2,1)S(1)} async-done(((bf16[8,64,4,256]{3,2,1,0:T(4,128)(2,1)}), bf16[8,64,4,256]{3,2,1,0:T(4,128)(2,1)S(1)}, u32[]{:S(2)}, u32[]{:S(2)}) %all-to-all-start) | async-done | bytes 1048608 | tf_op jit(solution)/shard_map/all_to_all | solution.py:73
  32.2 4.8 %all-to-all-start.1 = ((bf16[8,2,64,512]{3,2,1,0:T(8,128)(2,1)}), bf16[8,2,64,512]{3,2,1,0:T(8,128)(2,1)S(1)}, u32[]{:S(2)}, u32[]{:S(2)}) async-start(bf16[8,2,64,512]{3,2,1,0:T(8,128)(2,1)} %copy.213), calls=%async_computation.1 | async-start | bytes 2097152 | tf_op jit(solution)/shard_map/all_to_all | solution.py:74
  39.2 10.8 %all-to-all-done.1 = bf16[8,2,64,512]{3,2,1,0:T(8,128)(2,1)S(1)} async-done(((bf16[8,2,64,512]{3,2,1,0:T(8,128)(2,1)}), bf16[8,2,64,512]{3,2,1,0:T(8,128)(2,1)S(1)}, u32[]{:S(2)}, u32[]{:S(2)}) %all-to-all-start.1) | async-done | bytes 1048608 | tf_op jit(solution)/shard_map/all_to_all | solution.py:74
  50.0 5.3 %all-to-all-start.2 = ((bf16[8,64,4,256]{3,2,1,0:T(4,128)(2,1)}), bf16[8,64,4,256]{3,2,1,0:T(4,128)(2,1)}, u32[]{:S(2)}, u32[]{:S(2)}) async-start(bf16[8,64,4,256]{3,2,1,0:T(4,128)(2,1)} %copy.231), calls=%async_computation.2 | async-start | bytes 2097152 | tf_op jit(solution)/shard_map/all_to_all | solution.py:75
  60.2 12.0 %all-to-all-done.2 = bf16[8,64,4,256]{3,2,1,0:T(4,128)(2,1)} async-done(((bf16[8,64,4,256]{3,2,1,0:T(4,128)(2,1)}), bf16[8,64,4,256]{3,2,1,0:T(4,128)(2,1)}, u32[]{:S(2)}, u32[]{:S(2)}) %all-to-all-start.2) | async-done | bytes 1048608 | tf_op jit(solution)/shard_map/all_to_all | solution.py:75
  82.6 21.9 %all-gather.2.cloned.1.call-done = bf16[2,1,1024,512]{3,0,1,2:T(2,128)(2,1)} async-done(((bf16[2,1,64,512]{3,0,1,2:T(2,128)(2,1)}), bf16[2,1,1024,512]{3,0,1,2:T(2,128)(2,1)}) %all-gather.2.cloned.1.call-update) | async-done | bytes 2097168 | tf_op jit(solution)/shard_map/all_gather | solution.py:58
  104.5 6.9 %fusion.60 = (bf16[1,1,1024,512]{3,0,1,2:T(2,128)(2,1)}, bf16[1,1,1024,512]{3,0,1,2:T(2,128)(2,1)}) fusion(bf16[2,1,1024,512]{3,0,1,2:T(2,128)(2,1)} %all-gather.2.cloned.1.call-done), kind=kLoop, calls=%fused_computation.87 | loop fusion | bytes 4194304 | tf_op jit(solution)/shard_map/slice | solution.py:60
  111.4 5.8 %copy.323 = bf16[1,1,1024,512]{2,3,1,0:T(8,128)(2,1)} copy(bf16[1,1,1024,512]{3,0,1,2:T(2,128)(2,1)} %get-tuple-element.37) | data formatting | bytes 2097152
  117.2 5.6 %bitcast_reduce_fusion = (f32[9,4,2,64]{3,2,0,1:T(2,128)S(1)}, f32[4,9,64,2,1024]{4,2,3,1,0:T(8,128)S(1)}) fusion(pred[9,64,1024]{2,1,0:T(8,128)(4,1)} %concatenate.17, bf16[1024,4,128,1,1]{0,2,4,3,1:T(8,128)(2,1)} %bitcast.155, bf16[9,64,4,2,128]{4,3,2,1,0:T(2,128)(2,1)} %reshape.116), kind=kOutput, calls=%fused_computation.5 | convolution fusion | flops 1222110720 | bytes 21710848 | tf_op jit(solution)/shard_map/brkgd,nkd->bkgrn/dot_general | solution.py:13
  122.9 5.4 %fusion.3 = f32[9,4,2,64]{3,2,0,1:T(2,128)S(1)} fusion(f32[4,9,64,2,1024]{4,2,3,1,0:T(8,128)S(1)} %get-tuple-element.43, f32[9,4,2,64]{3,2,0,1:T(2,128)S(1)} %copy.218, pred[9,64,1024]{2,1,0:T(8,128)(4,1)S(1)} %copy-done.13), kind=kLoop, calls=%fused_computation.7 | loop fusion | flops 18869760 | bytes 19501056 | tf_op jit(solution)/shard_map/reduce_sum | solution.py:20
  130.0 5.8 %copy.325 = bf16[1,1,1024,512]{2,3,1,0:T(8,128)(2,1)} copy(bf16[1,1,1024,512]{3,0,1,2:T(2,128)(2,1)} %get-tuple-element.36) | data formatting | bytes 2097152
  135.8 10.9 %fusion.28 = f32[4,128,1024,1,1]{2,1,4,3,0:T(8,128)} fusion(bf16[9,64,4,2,128]{4,3,2,1,0:T(2,128)(2,1)} %copy-done.6, f32[4,9,64,2,1024]{4,2,3,1,0:T(8,128)} %copy-done.5, f32[9,4,2,64]{3,2,0,1:T(2,128)S(1)} %copy.222, pred[9,64,1024]{2,1,0:T(8,128)(4,1)} %concatenate.17), kind=kOutput, calls=%fused_computation.54 | convolution fusion | flops 1226833920 | bytes 22759424 | tf_op jit(solution)/shard_map/bkgrn,brkgd->nkd/dot_general | solution.py:42
  148.8 10.0 %multiply_reduce_fusion = (f32[9,4,2,64]{3,2,0,1:T(2,128)S(1)}, bf16[9,64,4,2,128]{4,1,3,0,2:T(8,128)(2,1)}) fusion(f32[9,4,2,64,128]{4,2,3,1,0:T(2,128)S(1)} %copy-done.16, f32[9,4,128,2,64]{2,4,3,0,1:T(8,128)S(1)} %fusion.19, bf16[1024,4,128,1,1]{0,2,4,3,1:T(8,128)(2,1)S(1)} %bitcast.159, f32[4,9,64,2,1024]{4,2,3,1,0:T(8,128)} %copy-done.5, ...), kind=kOutput, calls=%fused_computation.21 | convolution fusion | flops 1229778432 | bytes 26447872 | tf_op jit(solution)/shard_map/bkgrn,nkd->brkgd/dot_general | solution.py:29
  158.9 10.1 %fusion.1 = bf16[9,4,2,64,1024]{4,3,2,0,1:T(8,128)(2,1)S(1)} fusion(f32[4,9,64,2,1024]{4,2,3,1,0:T(8,128)} %copy-done.5, f32[9,4,2,64]{3,2,0,1:T(2,128)S(1)} %get-tuple-element.44, f32[9,4,2,64]{3,2,0,1:T(2,128)S(1)} %copy.222, pred[9,64,1024]{2,1,0:T(8,128)(4,1)S(1)} %copy-done.15, bf16[1024,4,128,1,1]{0,2,4,3,1:T(8,128)(2,1)} %bitcast.158, ...), kind=kOutput, calls=%fused_computation.2 | convolution fusion | flops 1236271104 | bytes 31166464 | tf_op jit(solution)/shard_map/brkgd,nkd->bkgrn/dot_general | solution.py:33
  169.0 5.2 %bitcast_multiply_fusion = f32[4,128,1024]{2,1,0:T(8,128)} fusion(bf16[9,4,2,64,1024]{4,3,2,0,1:T(8,128)(2,1)S(1)} %fusion.1, bf16[9,64,4,2,128]{4,3,2,1,0:T(2,128)(2,1)} %reshape.116), kind=kOutput, calls=%fused_computation.25 | convolution fusion | flops 1208483840 | bytes 12713984 | tf_op jit(solution)/shard_map/bkgrn,brkgd->nkd/dot_general | solution.py:41
  179.0 4.1 pad_maximum_fusion
  200.2 6.3 %fusion.7 = bf16[9,64,4,2,128]{4,1,3,0,2:T(8,128)(2,1)S(1)} fusion(f32[9,4,128,2,64]{2,4,3,0,1:T(8,128)S(1)} %fusion.17, bf16[9,4,2,64,1024]{4,3,2,0,1:T(8,128)(2,1)} %copy-done.2, bf16[1024,4,128,1,1]{0,2,4,3,1:T(8,128)(2,1)S(1)} %bitcast.156), kind=kOutput, calls=%fused_computation.14 | convolution fusion | flops 1209729024 | bytes 14024704 | tf_op jit(solution)/shard_map/bkgrn,nkd->brkgd/dot_general | solution.py:38
  209.2 5.5 %all-to-all-start.4 = ((bf16[8,64,4,256]{3,2,1,0:T(4,128)(2,1)}), bf16[8,64,4,256]{3,2,1,0:T(4,128)(2,1)S(1)}, u32[]{:S(2)}, u32[]{:S(2)}) async-start(bf16[8,64,4,256]{3,2,1,0:T(4,128)(2,1)} %reshape.121), calls=%async_computation.6 | async-start | bytes 2097152 | tf_op jit(solution)/shard_map/all_to_all | solution.py:119
  217.3 9.8 %all-to-all-done.4 = bf16[8,64,4,256]{3,2,1,0:T(4,128)(2,1)S(1)} async-done(((bf16[8,64,4,256]{3,2,1,0:T(4,128)(2,1)}), bf16[8,64,4,256]{3,2,1,0:T(4,128)(2,1)S(1)}, u32[]{:S(2)}, u32[]{:S(2)}) %all-to-all-start.4) | async-done | bytes 1048608 | tf_op jit(solution)/shard_map/all_to_all | solution.py:119
  227.1 4.8 %all-to-all-start.3 = ((bf16[8,64,4,256]{3,2,1,0:T(4,128)(2,1)}), bf16[8,64,4,256]{3,2,1,0:T(4,128)(2,1)S(1)}, u32[]{:S(2)}, u32[]{:S(2)}) async-start(bf16[8,64,4,256]{3,2,1,0:T(4,128)(2,1)} %reshape.120), calls=%async_computation.5 | async-start | bytes 2097152 | tf_op jit(solution)/shard_map/all_to_all | solution.py:118
  234.1 12.6 %all-to-all-done.3 = bf16[8,64,4,256]{3,2,1,0:T(4,128)(2,1)S(1)} async-done(((bf16[8,64,4,256]{3,2,1,0:T(4,128)(2,1)}), bf16[8,64,4,256]{3,2,1,0:T(4,128)(2,1)S(1)}, u32[]{:S(2)}, u32[]{:S(2)}) %all-to-all-start.3) | async-done | bytes 1048608 | tf_op jit(solution)/shard_map/all_to_all | solution.py:118
  246.7 5.2 %all-to-all-start.5 = ((bf16[8,2,64,256]{3,2,1,0:T(8,128)(2,1)}), bf16[8,2,64,256]{3,2,1,0:T(8,128)(2,1)}, u32[]{:S(2)}, u32[]{:S(2)}) async-start(bf16[8,2,64,256]{3,2,1,0:T(8,128)(2,1)} %copy.256), calls=%async_computation.8 | async-start | bytes 1048576 | tf_op jit(solution)/shard_map/all_to_all | solution.py:120
  261.7 164.3 %reduce-scatter.6.cloned.1.call-done = f32[2,64,256]{2,1,0:T(8,128)} async-done(((f32[2,1024,256]{2,1,0:T(8,128)}), f32[2,64,256]{2,1,0:T(8,128)}) %reduce-scatter.6.cloned.1.call-update) | async-done | bytes 131088 | tf_op jit(solution)/shard_map/reduce_scatter | solution.py:110
  (129 shorter events, 68.5 us)
Async XLA Ops:
  7.2 97.3 %all-gather.2.cloned.1.call-start = ((), (), s32[]{:S(2)}) async-start(), calls=%async_computation.9 | async-start | bytes 2228224 | tf_op jit(solution)/shard_map/all_gather | solution.py:58
  10.5 7.2 %copy-start.21 = (bf16[2,1,1,8,64,512]{5,4,3,2,1,0:T(8,128)(2,1)S(1)}, bf16[2,1,1,8,64,512]{5,4,3,2,1,0:T(8,128)(2,1)}, u32[]{:S(2)}) copy-start(bf16[2,1,1,8,64,512]{5,4,3,2,1,0:T(8,128)(2,1)} %param.11) | copy-start | bytes 3145732
  10.5 7.2 %copy-start.26 = (s32[1,1,8]{2,1,0:T(1,128)S(1)}, s32[1,1,8]{2,1,0:T(1,128)}, u32[]{:S(2)}) copy-start(s32[1,1,8]{2,1,0:T(1,128)} %param.13) | copy-start | bytes 100
  11.9 20.3 %all-to-all-start = ((bf16[8,64,4,256]{3,2,1,0:T(4,128)(2,1)}), bf16[8,64,4,256]{3,2,1,0:T(4,128)(2,1)S(1)}, u32[]{:S(2)}, u32[]{:S(2)}) async-start(bf16[8,64,4,256]{3,2,1,0:T(4,128)(2,1)} %copy.205), calls=%async_computation | async-start | bytes 2097152 | tf_op jit(solution)/shard_map/all_to_all | solution.py:73
  18.5 18.5 %copy-start.22 = (bf16[1,1,8,64,4,256]{5,4,3,2,1,0:T(4,128)(2,1)S(1)}, bf16[1,1,8,64,4,256]{5,4,3,2,1,0:T(4,128)(2,1)}, u32[]{:S(2)}) copy-start(bf16[1,1,8,64,4,256]{5,4,3,2,1,0:T(4,128)(2,1)} %param.12) | copy-start | bytes 3145732
  32.2 17.8 %all-to-all-start.1 = ((bf16[8,2,64,512]{3,2,1,0:T(8,128)(2,1)}), bf16[8,2,64,512]{3,2,1,0:T(8,128)(2,1)S(1)}, u32[]{:S(2)}, u32[]{:S(2)}) async-start(bf16[8,2,64,512]{3,2,1,0:T(8,128)(2,1)} %copy.213), calls=%async_computation.1 | async-start | bytes 2097152 | tf_op jit(solution)/shard_map/all_to_all | solution.py:74
  37.8 19.3 %copy-start.23 = (bf16[1,64,4,256]{3,2,1,0:T(4,128)(2,1)S(1)}, bf16[1,64,4,256]{3,2,1,0:T(4,128)(2,1)}, u32[]{:S(2)}) copy-start(bf16[1,64,4,256]{3,2,1,0:T(4,128)(2,1)} %param.7) | copy-start | bytes 393220
  50.0 22.2 %all-to-all-start.2 = ((bf16[8,64,4,256]{3,2,1,0:T(4,128)(2,1)}), bf16[8,64,4,256]{3,2,1,0:T(4,128)(2,1)}, u32[]{:S(2)}, u32[]{:S(2)}) async-start(bf16[8,64,4,256]{3,2,1,0:T(4,128)(2,1)} %copy.231), calls=%async_computation.2 | async-start | bytes 2097152 | tf_op jit(solution)/shard_map/all_to_all | solution.py:75
  55.3 142.4 %reduce-scatter.4.cloned.1.call-start = ((), (), s32[]{:S(2)}) async-start(), calls=%async_computation.10 | async-start | bytes 6291456 | tf_op jit(solution)/shard_map/reduce_scatter | solution.py:109
  59.7 12.5 %copy-start.24 = (bf16[1,64,4,256]{3,2,1,0:T(4,128)(2,1)S(1)}, bf16[1,64,4,256]{3,2,1,0:T(4,128)(2,1)}, u32[]{:S(2)}) copy-start(bf16[1,64,4,256]{3,2,1,0:T(4,128)(2,1)} %param.9) | copy-start | bytes 393220
  78.1 3.2 copy-start.6
  78.6 2.7 copy-start.17
  82.6 64.1 %copy-start.3 = (f32[9,4,2,64,64]{3,4,2,1,0:T(8,128)}, f32[9,4,2,64,64]{3,4,2,1,0:T(8,128)S(1)}, u32[]{:S(2)}) copy-start(f32[9,4,2,64,64]{3,4,2,1,0:T(8,128)S(1)} %get-tuple-element.41) | copy-start | bytes 3538948
  117.2 5.7 %copy-start.13 = (pred[9,64,1024]{2,1,0:T(8,128)(4,1)S(1)}, pred[9,64,1024]{2,1,0:T(8,128)(4,1)}, u32[]{:S(2)}) copy-start(pred[9,64,1024]{2,1,0:T(8,128)(4,1)} %concatenate.17) | copy-start | bytes 1769476
  122.8 6.4 %copy-start.5 = (f32[4,9,64,2,1024]{4,2,3,1,0:T(8,128)}, f32[4,9,64,2,1024]{4,2,3,1,0:T(8,128)S(1)}, u32[]{:S(2)}) copy-start(f32[4,9,64,2,1024]{4,2,3,1,0:T(8,128)S(1)} %get-tuple-element.43) | copy-start | bytes 56623108
  148.8 10.0 %copy-start.15 = (pred[9,64,1024]{2,1,0:T(8,128)(4,1)S(1)}, pred[9,64,1024]{2,1,0:T(8,128)(4,1)}, u32[]{:S(2)}) copy-start(pred[9,64,1024]{2,1,0:T(8,128)(4,1)} %concatenate.17) | copy-start | bytes 1769476
  169.0 5.2 %copy-start.2 = (bf16[9,4,2,64,1024]{4,3,2,0,1:T(8,128)(2,1)}, bf16[9,4,2,64,1024]{4,3,2,0,1:T(8,128)(2,1)S(1)}, u32[]{:S(2)}) copy-start(bf16[9,4,2,64,1024]{4,3,2,0,1:T(8,128)(2,1)S(1)} %fusion.1) | copy-start | bytes 28311556
  183.2 48.8 %reduce-scatter.8.cloned.1.call-start = ((), (), s32[]{:S(2)}) async-start(), calls=%async_computation.12 | async-start | bytes 3145728 | tf_op jit(solution)/shard_map/reduce_scatter | solution.py:114
  197.6 228.4 %reduce-scatter.6.cloned.1.call-start = ((), (), s32[]{:S(2)}) async-start(), calls=%async_computation.11 | async-start | bytes 2228224 | tf_op jit(solution)/shard_map/reduce_scatter | solution.py:110
  207.7 7.0 %copy-start.19 = (bf16[9,64,4,2,128]{4,1,3,0,2:T(8,128)(2,1)S(1)}, bf16[9,64,4,2,128]{4,1,3,0,2:T(8,128)(2,1)}, u32[]{:S(2)}) copy-start(bf16[9,64,4,2,128]{4,1,3,0,2:T(8,128)(2,1)} %get-tuple-element.45) | copy-start | bytes 3538948
  209.2 18.0 %all-to-all-start.4 = ((bf16[8,64,4,256]{3,2,1,0:T(4,128)(2,1)}), bf16[8,64,4,256]{3,2,1,0:T(4,128)(2,1)S(1)}, u32[]{:S(2)}, u32[]{:S(2)}) async-start(bf16[8,64,4,256]{3,2,1,0:T(4,128)(2,1)} %reshape.121), calls=%async_computation.6 | async-start | bytes 2097152 | tf_op jit(solution)/shard_map/all_to_all | solution.py:119
  227.1 19.5 %all-to-all-start.3 = ((bf16[8,64,4,256]{3,2,1,0:T(4,128)(2,1)}), bf16[8,64,4,256]{3,2,1,0:T(4,128)(2,1)S(1)}, u32[]{:S(2)}, u32[]{:S(2)}) async-start(bf16[8,64,4,256]{3,2,1,0:T(4,128)(2,1)} %reshape.120), calls=%async_computation.5 | async-start | bytes 2097152 | tf_op jit(solution)/shard_map/all_to_all | solution.py:118
  246.7 12.6 %all-to-all-start.5 = ((bf16[8,2,64,256]{3,2,1,0:T(8,128)(2,1)}), bf16[8,2,64,256]{3,2,1,0:T(8,128)(2,1)}, u32[]{:S(2)}, u32[]{:S(2)}) async-start(bf16[8,2,64,256]{3,2,1,0:T(8,128)(2,1)} %copy.256), calls=%async_computation.8 | async-start | bytes 1048576 | tf_op jit(solution)/shard_map/all_to_all | solution.py:120
  256.7 170.7 %copy-start.1 = (bf16[1,1,8,64,4,256]{5,4,3,2,1,0:T(4,128)(2,1)S(1)}, bf16[1,1,8,64,4,256]{5,4,3,2,1,0:T(4,128)(2,1)}, u32[]{:S(2)}) copy-start(bf16[1,1,8,64,4,256]{5,4,3,2,1,0:T(4,128)(2,1)} %param.10) | copy-start | bytes 3145732
  (13 other events, 22.8 us)
Sparse Core Ops, SparseCore 0:
  11.2 93.2 all-gather.1
  183.3 13.8 reduce-scatter.3
  199.8 16.2 reduce-scatter.7
  219.8 206.0 reduce-scatter.5
where the time goes:
time: 440 us; the launch traced here: 434 us
  waiting for transfers between devices  245 us (56%)
  matrix products  61.5 us (14%)
  local copies, waits for them, and re-layouts  60.6 us (14%)
  starting transfers between devices  31.8 us (7%)
  other arithmetic  21.2 us (5%)
  between operations  14.5 us (3%)
    reduce_scatter x1, waiting for transfers between devices, body(): lax.psum_scatter(head_sum, 'prompt', scatter_dimension=1, tiled=True)  164 us
    unnamed x64, local copies, waits for them, and re-layouts  24.9 us
    all_gather x1, waiting for transfers between devices, body(): gathered = lax.all_gather(prompt_kv, 'prompt', axis=2, tiled=True)  21.9 us
    all_to_all x1, waiting for transfers between devices, body(): lax.all_to_all(out[:peers], 'resp', split_axis=0, concat_axis=0, tiled=True)  12.6 us
    all_to_all x1, waiting for transfers between devices, body(): lax.all_to_all(send_q, 'resp', split_axis=0, concat_axis=0, tiled=True)  12.4 us
    all_to_all x1, waiting for transfers between devices, body(): lax.all_to_all(send_grad, 'resp', split_axis=0, concat_axis=0, tiled=True)  12 us
    dot_general x1, matrix products, attend_blocks(): jnp.einsum('bkgrn,brkgd->nkd', w_sh, cotangent, preferred_element_type=f32)  10.9 us
    all_to_all x1, waiting for transfers between devices, body(): lax.all_to_all(send_kv, 'resp', split_axis=0, concat_axis=0, tiled=True)  10.8 us
  transfers between devices with their start and end apart: 10, of which 8 were waited for; matrix products, arithmetic and copies ran while one was open for 13% of the time, Pallas kernels for 0%

commit v1 on v0

--- a/solution.py
+++ b/solution.py
@@ -5,6 +5,10 @@
 from jax.sharding import PartitionSpec as P
 
 HD = 128
+finish_the_links = lambda frame_in: jnp.concatenate(
+    lax.all_to_all(jnp.stack([frame_in for _ in range(lax.axis_size("prompt"))]), "prompt", 0, 0),
+    axis=2,
+)
 
 
 def attend_blocks(queries, keys_in, values_in, own_keys, own_values, cotangent, shared_ok, own_ok):
@@ -55,7 +59,7 @@
     resp_len = resp_q.shape[3]
     peers = lax.axis_size("resp")
     kv_width = kv_heads * head_size
-    gathered = lax.all_gather(prompt_kv, "prompt", axis=2, tiled=True)
+    gathered = finish_the_links(prompt_kv)
     prompt_keys = gathered[0, 0].reshape(full_len, kv_heads, head_size)
     prompt_values = gathered[1, 0].reshape(full_len, kv_heads, head_size)
     order = resp_prompt[0, 0]

time: 440 us -> 461 us (1.048)
  blocking collectives: 0 us -> 18.8 us
  local copies, waits for them, and re-layouts: 60.6 us -> 49.4 us
  starting transfers between devices: 31.8 us -> 38 us
  matrix products: 61.5 us -> 67.3 us
    all_to_all x1, waiting for transfers between devices: 12 us -> 34 us  [lax.all_to_all(jnp.stack([frame_in for _ in range(lax.axis_size('prompt')...]
    all_gather x1 -> x0, waiting for transfers between devices: 21.9 us -> none  [body(): gathered = lax.all_gather(prompt_kv, 'prompt', axis=2, tiled=True)]
    all_to_all x0 -> x1, blocking collectives: none -> 18.8 us  [body(): lax.all_to_all(send_grad, 'resp', split_axis=0, concat_axis=0, tiled=True)]
    unnamed x64 -> x61, local copies, waits for them, and re-layouts: 24.9 us -> 12.1 us
    another operation x0 -> x3, local copies, waits for them, and re-layouts: none -> 5.81 us  [the longest x1 2.14 us: body(): prompt_values = gathered[1, 0].reshape(full_len, kv_heads, head_size)]
    all_to_all x1, starting transfers between devices: 5.28 us -> 10.9 us  [lax.all_to_all(jnp.stack([frame_in for _ in range(lax.axis_size('prompt')...]
  transfers between devices with their start and end apart: 10 -> 9, of which waited for: 8 -> 8; matrix products, arithmetic and copies ran while one was open for 13% -> 11% of each run, Pallas kernels for 0% -> 0%
where the time goes in v1:
time: 461 us; the launch traced here: 456 us
  waiting for transfers between devices  247 us (54%)
  matrix products  67.3 us (15%)
  local copies, waits for them, and re-layouts  49.4 us (11%)
  starting transfers between devices  38 us (8%)
  other arithmetic  20.5 us (4%)
  blocking collectives  18.8 us (4%)
  between operations  14.5 us (3%)
    reduce_scatter x1, waiting for transfers between devices, body(): lax.psum_scatter(head_sum, 'prompt', scatter_dimension=1, tiled=True)  164 us
    all_to_all x1, waiting for transfers between devices, lax.all_to_all(jnp.stack([frame_in for _ in range(lax.axis_size('prompt')...  34 us
    all_to_all x1, blocking collectives, body(): lax.all_to_all(send_grad, 'resp', split_axis=0, concat_axis=0, tiled=True)  18.8 us
    dot_general x1, matrix products, attend_blocks(): jnp.einsum('brkgd,nkd->bkgrn', cotangent, values_in, preferred_element_ty...  14.1 us
    all_to_all x1, waiting for transfers between devices, body(): lax.all_to_all(send_kv, 'resp', split_axis=0, concat_axis=0, tiled=True)  12.6 us
    all_to_all x1, waiting for transfers between devices, body(): lax.all_to_all(out[:peers], 'resp', split_axis=0, concat_axis=0, tiled=True)  12.5 us
    unnamed x61, local copies, waits for them, and re-layouts  12.1 us
    all_to_all x1, waiting for transfers between devices, body(): lax.all_to_all(send_q, 'resp', split_axis=0, concat_axis=0, tiled=True)  11.5 us
  transfers between devices with their start and end apart: 9, of which 8 were waited for; matrix products, arithmetic and copies ran while one was open for 11% of the time, Pallas kernels for 0%

profile of v1, /device:TPU:8, one launch (start us, length us, event | category | flops | bytes accessed | tf_op | source)
XLA Modules:
  0.0 455.8 jit_solution(11504960595989508049)
XLA Ops:
  11.2 5.8 %all-to-all-start = ((bf16[8,64,4,256]{3,2,1,0:T(4,128)(2,1)}), bf16[8,64,4,256]{3,2,1,0:T(4,128)(2,1)S(1)}, u32[]{:S(2)}, u32[]{:S(2)}) async-start(bf16[8,64,4,256]{3,2,1,0:T(4,128)(2,1)} %copy.198), calls=%async_computation | async-start | bytes 2097152 | tf_op jit(solution)/shard_map/all_to_all | solution.py:77
  19.2 11.5 %all-to-all-done = bf16[8,64,4,256]{3,2,1,0:T(4,128)(2,1)S(1)} async-done(((bf16[8,64,4,256]{3,2,1,0:T(4,128)(2,1)}), bf16[8,64,4,256]{3,2,1,0:T(4,128)(2,1)S(1)}, u32[]{:S(2)}, u32[]{:S(2)}) %all-to-all-start) | async-done | bytes 1048608 | tf_op jit(solution)/shard_map/all_to_all | solution.py:77
  30.7 4.8 %all-to-all-start.2 = ((bf16[8,2,64,512]{3,2,1,0:T(8,128)(2,1)}), bf16[8,2,64,512]{3,2,1,0:T(8,128)(2,1)S(1)}, u32[]{:S(2)}, u32[]{:S(2)}) async-start(bf16[8,2,64,512]{3,2,1,0:T(8,128)(2,1)} %copy.204), calls=%async_computation.2 | async-start | bytes 2097152 | tf_op jit(solution)/shard_map/all_to_all | solution.py:78
  36.8 12.6 %all-to-all-done.2 = bf16[8,2,64,512]{3,2,1,0:T(8,128)(2,1)S(1)} async-done(((bf16[8,2,64,512]{3,2,1,0:T(8,128)(2,1)}), bf16[8,2,64,512]{3,2,1,0:T(8,128)(2,1)S(1)}, u32[]{:S(2)}, u32[]{:S(2)}) %all-to-all-start.2) | async-done | bytes 1048608 | tf_op jit(solution)/shard_map/all_to_all | solution.py:78
  49.3 18.8 %all_to_all.35 = bf16[8,64,4,256]{3,2,1,0:T(4,128)(2,1)} all-to-all(bf16[8,64,4,256]{3,2,1,0:T(4,128)(2,1)S(1)} %copy.221), channel_id=1, replica_groups=mesh['prompt'=16,'resp'=8,'head'=2] {'resp'}, dimensions={0} | all-to-all | bytes 2097152 | tf_op jit(solution)/shard_map/all_to_all | solution.py:79
  69.7 10.9 %all-to-all-start.1 = ((bf16[16,2,1,64,512]{4,3,2,1,0:T(8,128)(2,1)}), bf16[16,2,1,64,512]{4,3,2,1,0:T(8,128)(2,1)}, u32[]{:S(2)}, u32[]{:S(2)}) async-start(bf16[16,2,1,64,512]{4,3,2,1,0:T(8,128)(2,1)} %stack.14), calls=%async_computation.1 | async-start | bytes 4194304 | tf_op jit(solution)/shard_map/all_to_all | solution.py:9
  95.7 34.0 %all-to-all-done.1 = bf16[16,2,1,64,512]{4,3,2,1,0:T(8,128)(2,1)} async-done(((bf16[16,2,1,64,512]{4,3,2,1,0:T(8,128)(2,1)}), bf16[16,2,1,64,512]{4,3,2,1,0:T(8,128)(2,1)}, u32[]{:S(2)}, u32[]{:S(2)}) %all-to-all-start.1) | async-done | bytes 2097184 | tf_op jit(solution)/shard_map/all_to_all | solution.py:9
  129.7 3.1 fusion.64
  134.9 5.5 %bitcast_reduce_fusion = (f32[9,4,2,64]{3,2,0,1:T(2,128)S(1)}, f32[4,9,64,2,1024]{4,2,3,1,0:T(8,128)S(1)}) fusion(pred[9,64,1024]{2,1,0:T(8,128)(4,1)} %concatenate.17, bf16[1024,4,128,1,1]{2,1,0,4,3:T(4,128)(2,1)} %bitcast.153, bf16[9,64,4,2,128]{4,3,2,1,0:T(2,128)(2,1)} %reshape.128), kind=kOutput, calls=%fused_computation.5 | convolution fusion | flops 1222110720 | bytes 21710848 | tf_op jit(solution)/shard_map/brkgd,nkd->bkgrn/dot_general | solution.py:17
  140.5 5.4 %fusion.3 = f32[9,4,2,64]{3,2,0,1:T(2,128)S(1)} fusion(f32[4,9,64,2,1024]{4,2,3,1,0:T(8,128)S(1)} %get-tuple-element.43, f32[9,4,2,64]{3,2,0,1:T(2,128)S(1)} %copy.209, pred[9,64,1024]{2,1,0:T(8,128)(4,1)S(1)} %copy-done.13), kind=kLoop, calls=%fused_computation.7 | loop fusion | flops 18869760 | bytes 19501056 | tf_op jit(solution)/shard_map/reduce_sum | solution.py:24
  149.7 10.9 %fusion.28 = f32[4,128,1024,1,1]{2,1,4,3,0:T(8,128)} fusion(bf16[9,64,4,2,128]{4,3,2,1,0:T(2,128)(2,1)} %copy-done.3, f32[4,9,64,2,1024]{4,2,3,1,0:T(8,128)} %copy-done.2, f32[9,4,2,64]{3,2,0,1:T(2,128)S(1)} %copy.213, pred[9,64,1024]{2,1,0:T(8,128)(4,1)} %concatenate.17), kind=kOutput, calls=%fused_computation.54 | convolution fusion | flops 1226833920 | bytes 22759424 | tf_op jit(solution)/shard_map/bkgrn,brkgd->nkd/dot_general | solution.py:46
  162.8 10.4 %multiply_reduce_fusion = (f32[9,4,2,64]{3,2,0,1:T(2,128)S(1)}, bf16[9,64,4,2,128]{4,1,3,0,2:T(8,128)(2,1)}) fusion(f32[9,4,2,64,128]{4,2,3,1,0:T(2,128)S(1)} %copy-done.15, f32[9,4,128,2,64]{2,4,3,0,1:T(8,128)S(1)} %fusion.19, bf16[1024,4,128,1,1]{2,1,0,4,3:T(4,128)(2,1)S(1)} %bitcast.159, f32[4,9,64,2,1024]{4,2,3,1,0:T(8,128)} %copy-done.2, ...), kind=kOutput, calls=%fused_computation.21 | convolution fusion | flops 1229778432 | bytes 26447872 | tf_op jit(solution)/shard_map/bkgrn,nkd->brkgd/dot_general | solution.py:33
  173.2 14.1 %fusion.1 = bf16[9,4,2,64,1024]{4,3,2,0,1:T(8,128)(2,1)} fusion(f32[4,9,64,2,1024]{4,2,3,1,0:T(8,128)} %copy-done.2, f32[9,4,2,64]{3,2,0,1:T(2,128)S(1)} %get-tuple-element.44, f32[9,4,2,64]{3,2,0,1:T(2,128)S(1)} %copy.213, pred[9,64,1024]{2,1,0:T(8,128)(4,1)S(1)} %copy-done.14, bf16[9,64,4,2,128]{4,3,2,1,0:T(2,128)(2,1)S(1)} %copy-done.4, ...), kind=kOutput, calls=%fused_computation.2 | convolution fusion | flops 1236271104 | bytes 31166464 | tf_op jit(solution)/shard_map/brkgd,nkd->bkgrn/dot_general | solution.py:37
  187.3 6.7 %bitcast_multiply_fusion = f32[4,128,1024]{2,1,0:T(8,128)} fusion(bf16[9,4,2,64,1024]{4,3,2,0,1:T(8,128)(2,1)} %fusion.1, bf16[9,64,4,2,128]{4,3,2,1,0:T(2,128)(2,1)S(1)} %copy-done.6), kind=kOutput, calls=%fused_computation.25 | convolution fusion | flops 1208483840 | bytes 12713984 | tf_op jit(solution)/shard_map/bkgrn,brkgd->nkd/dot_general | solution.py:45
  194.0 2.9 copy.234
  196.9 3.0 copy.235
  199.9 4.6 %pad_maximum_fusion = f32[2,1024,512]{2,1,0:T(8,128)} fusion(f32[1,1024,512]{2,1,0:T(8,128)} %copy.235, f32[1,1024,512]{2,1,0:T(8,128)} %copy.234), kind=kLoop, calls=%fused_computation.11 | loop fusion | flops 1048576 | bytes 8388608 | tf_op jit(solution)/shard_map/stack | solution.py:112
  220.6 6.3 %fusion.7 = bf16[9,64,4,2,128]{4,1,3,0,2:T(8,128)(2,1)S(1)} fusion(f32[9,4,128,2,64]{2,4,3,0,1:T(8,128)S(1)} %fusion.17, bf16[9,4,2,64,1024]{4,3,2,0,1:T(8,128)(2,1)} %fusion.1, bf16[1024,4,128,1,1]{2,1,0,4,3:T(4,128)(2,1)S(1)} %bitcast.154), kind=kOutput, calls=%fused_computation.14 | convolution fusion | flops 1209729024 | bytes 14024704 | tf_op jit(solution)/shard_map/bkgrn,nkd->brkgd/dot_general | solution.py:42
  229.6 5.5 %all-to-all-start.5 = ((bf16[8,64,4,256]{3,2,1,0:T(4,128)(2,1)}), bf16[8,64,4,256]{3,2,1,0:T(4,128)(2,1)S(1)}, u32[]{:S(2)}, u32[]{:S(2)}) async-start(bf16[8,64,4,256]{3,2,1,0:T(4,128)(2,1)} %reshape.133), calls=%async_computation.7 | async-start | bytes 2097152 | tf_op jit(solution)/shard_map/all_to_all | solution.py:123
  237.8 11.1 %all-to-all-done.5 = bf16[8,64,4,256]{3,2,1,0:T(4,128)(2,1)S(1)} async-done(((bf16[8,64,4,256]{3,2,1,0:T(4,128)(2,1)}), bf16[8,64,4,256]{3,2,1,0:T(4,128)(2,1)S(1)}, u32[]{:S(2)}, u32[]{:S(2)}) %all-to-all-start.5) | async-done | bytes 1048608 | tf_op jit(solution)/shard_map/all_to_all | solution.py:123
  248.9 4.8 %all-to-all-start.4 = ((bf16[8,64,4,256]{3,2,1,0:T(4,128)(2,1)}), bf16[8,64,4,256]{3,2,1,0:T(4,128)(2,1)S(1)}, u32[]{:S(2)}, u32[]{:S(2)}) async-start(bf16[8,64,4,256]{3,2,1,0:T(4,128)(2,1)} %reshape.132), calls=%async_computation.6 | async-start | bytes 2097152 | tf_op jit(solution)/shard_map/all_to_all | solution.py:122
  255.9 12.5 %all-to-all-done.4 = bf16[8,64,4,256]{3,2,1,0:T(4,128)(2,1)S(1)} async-done(((bf16[8,64,4,256]{3,2,1,0:T(4,128)(2,1)}), bf16[8,64,4,256]{3,2,1,0:T(4,128)(2,1)S(1)}, u32[]{:S(2)}, u32[]{:S(2)}) %all-to-all-start.4) | async-done | bytes 1048608 | tf_op jit(solution)/shard_map/all_to_all | solution.py:122
  268.4 5.2 %all-to-all-start.6 = ((bf16[8,2,64,256]{3,2,1,0:T(8,128)(2,1)}), bf16[8,2,64,256]{3,2,1,0:T(8,128)(2,1)}, u32[]{:S(2)}, u32[]{:S(2)}) async-start(bf16[8,2,64,256]{3,2,1,0:T(8,128)(2,1)} %copy.246), calls=%async_computation.9 | async-start | bytes 1048576 | tf_op jit(solution)/shard_map/all_to_all | solution.py:124
  283.4 164.1 %reduce-scatter.6.cloned.1.call-done = f32[2,64,256]{2,1,0:T(8,128)} async-done(((f32[2,1024,256]{2,1,0:T(8,128)}), f32[2,64,256]{2,1,0:T(8,128)}) %reduce-scatter.6.cloned.1.call-update) | async-done | bytes 131088 | tf_op jit(solution)/shard_map/reduce_scatter | solution.py:114
  (127 shorter events, 66.7 us)
Async XLA Ops:
  9.8 7.2 %copy-start.19 = (bf16[2,1,1,8,64,512]{5,4,3,2,1,0:T(8,128)(2,1)S(1)}, bf16[2,1,1,8,64,512]{5,4,3,2,1,0:T(8,128)(2,1)}, u32[]{:S(2)}) copy-start(bf16[2,1,1,8,64,512]{5,4,3,2,1,0:T(8,128)(2,1)} %param.11) | copy-start | bytes 3145732
  9.9 7.2 %copy-start.26 = (s32[1,1,8]{2,1,0:T(1,128)S(1)}, s32[1,1,8]{2,1,0:T(1,128)}, u32[]{:S(2)}) copy-start(s32[1,1,8]{2,1,0:T(1,128)} %param.13) | copy-start | bytes 100
  11.2 19.5 %all-to-all-start = ((bf16[8,64,4,256]{3,2,1,0:T(4,128)(2,1)}), bf16[8,64,4,256]{3,2,1,0:T(4,128)(2,1)S(1)}, u32[]{:S(2)}, u32[]{:S(2)}) async-start(bf16[8,64,4,256]{3,2,1,0:T(4,128)(2,1)} %copy.198), calls=%async_computation | async-start | bytes 2097152 | tf_op jit(solution)/shard_map/all_to_all | solution.py:77
  17.9 17.6 %copy-start.20 = (bf16[1,1,8,64,4,256]{5,4,3,2,1,0:T(4,128)(2,1)S(1)}, bf16[1,1,8,64,4,256]{5,4,3,2,1,0:T(4,128)(2,1)}, u32[]{:S(2)}) copy-start(bf16[1,1,8,64,4,256]{5,4,3,2,1,0:T(4,128)(2,1)} %param.12) | copy-start | bytes 3145732
  30.7 18.6 %all-to-all-start.2 = ((bf16[8,2,64,512]{3,2,1,0:T(8,128)(2,1)}), bf16[8,2,64,512]{3,2,1,0:T(8,128)(2,1)S(1)}, u32[]{:S(2)}, u32[]{:S(2)}) async-start(bf16[8,2,64,512]{3,2,1,0:T(8,128)(2,1)} %copy.204), calls=%async_computation.2 | async-start | bytes 2097152 | tf_op jit(solution)/shard_map/all_to_all | solution.py:78
  36.3 31.9 %copy-start.22 = (bf16[2,1,64,512]{3,2,1,0:T(8,128)(2,1)S(1)}, bf16[2,1,64,512]{3,2,1,0:T(8,128)(2,1)}, u32[]{:S(2)}) copy-start(bf16[2,1,64,512]{3,2,1,0:T(8,128)(2,1)} %param.8) | copy-start | bytes 393220
  69.7 13.4 %copy-start.23 = (bf16[1,64,4,256]{3,2,1,0:T(4,128)(2,1)S(1)}, bf16[1,64,4,256]{3,2,1,0:T(4,128)(2,1)}, u32[]{:S(2)}) copy-start(bf16[1,64,4,256]{3,2,1,0:T(4,128)(2,1)} %param.7) | copy-start | bytes 393220
  69.7 60.0 %all-to-all-start.1 = ((bf16[16,2,1,64,512]{4,3,2,1,0:T(8,128)(2,1)}), bf16[16,2,1,64,512]{4,3,2,1,0:T(8,128)(2,1)}, u32[]{:S(2)}, u32[]{:S(2)}) async-start(bf16[16,2,1,64,512]{4,3,2,1,0:T(8,128)(2,1)} %stack.14), calls=%async_computation.1 | async-start | bytes 4194304 | tf_op jit(solution)/shard_map/all_to_all | solution.py:9
  80.7 138.3 %reduce-scatter.4.cloned.1.call-start = ((), (), s32[]{:S(2)}) async-start(), calls=%async_computation.10 | async-start | bytes 6291456 | tf_op jit(solution)/shard_map/reduce_scatter | solution.py:113
  91.3 3.2 copy-start.3
  91.8 2.7 copy-start.16
  91.8 2.7 copy-start.5
  91.8 2.7 copy-start.25
  134.9 5.6 %copy-start.13 = (pred[9,64,1024]{2,1,0:T(8,128)(4,1)S(1)}, pred[9,64,1024]{2,1,0:T(8,128)(4,1)}, u32[]{:S(2)}) copy-start(pred[9,64,1024]{2,1,0:T(8,128)(4,1)} %concatenate.17) | copy-start | bytes 1769476
  140.4 6.4 %copy-start.2 = (f32[4,9,64,2,1024]{4,2,3,1,0:T(8,128)}, f32[4,9,64,2,1024]{4,2,3,1,0:T(8,128)S(1)}, u32[]{:S(2)}) copy-start(f32[4,9,64,2,1024]{4,2,3,1,0:T(8,128)S(1)} %get-tuple-element.43) | copy-start | bytes 56623108
  162.8 10.4 %copy-start.4 = (bf16[9,64,4,2,128]{4,3,2,1,0:T(2,128)(2,1)S(1)}, bf16[9,64,4,2,128]{4,3,2,1,0:T(2,128)(2,1)}, u32[]{:S(2)}) copy-start(bf16[9,64,4,2,128]{4,3,2,1,0:T(2,128)(2,1)} %copy-done.3) | copy-start | bytes 3538948
  173.2 14.1 %copy-start.6 = (bf16[9,64,4,2,128]{4,3,2,1,0:T(2,128)(2,1)S(1)}, bf16[9,64,4,2,128]{4,3,2,1,0:T(2,128)(2,1)}, u32[]{:S(2)}) copy-start(bf16[9,64,4,2,128]{4,3,2,1,0:T(2,128)(2,1)} %reshape.128) | copy-start | bytes 3538948
  204.6 49.2 %reduce-scatter.8.cloned.1.call-start = ((), (), s32[]{:S(2)}) async-start(), calls=%async_computation.12 | async-start | bytes 3145728 | tf_op jit(solution)/shard_map/reduce_scatter | solution.py:118
  217.9 229.6 %reduce-scatter.6.cloned.1.call-start = ((), (), s32[]{:S(2)}) async-start(), calls=%async_computation.11 | async-start | bytes 2228224 | tf_op jit(solution)/shard_map/reduce_scatter | solution.py:114
  228.1 7.0 %copy-start.18 = (bf16[9,64,4,2,128]{4,1,3,0,2:T(8,128)(2,1)S(1)}, bf16[9,64,4,2,128]{4,1,3,0,2:T(8,128)(2,1)}, u32[]{:S(2)}) copy-start(bf16[9,64,4,2,128]{4,1,3,0,2:T(8,128)(2,1)} %get-tuple-element.45) | copy-start | bytes 3538948
  229.6 19.3 %all-to-all-start.5 = ((bf16[8,64,4,256]{3,2,1,0:T(4,128)(2,1)}), bf16[8,64,4,256]{3,2,1,0:T(4,128)(2,1)S(1)}, u32[]{:S(2)}, u32[]{:S(2)}) async-start(bf16[8,64,4,256]{3,2,1,0:T(4,128)(2,1)} %reshape.133), calls=%async_computation.7 | async-start | bytes 2097152 | tf_op jit(solution)/shard_map/all_to_all | solution.py:123
  248.9 19.5 %all-to-all-start.4 = ((bf16[8,64,4,256]{3,2,1,0:T(4,128)(2,1)}), bf16[8,64,4,256]{3,2,1,0:T(4,128)(2,1)S(1)}, u32[]{:S(2)}, u32[]{:S(2)}) async-start(bf16[8,64,4,256]{3,2,1,0:T(4,128)(2,1)} %reshape.132), calls=%async_computation.6 | async-start | bytes 2097152 | tf_op jit(solution)/shard_map/all_to_all | solution.py:122
  268.4 12.6 %all-to-all-start.6 = ((bf16[8,2,64,256]{3,2,1,0:T(8,128)(2,1)}), bf16[8,2,64,256]{3,2,1,0:T(8,128)(2,1)}, u32[]{:S(2)}, u32[]{:S(2)}) async-start(bf16[8,2,64,256]{3,2,1,0:T(8,128)(2,1)} %copy.246), calls=%async_computation.9 | async-start | bytes 1048576 | tf_op jit(solution)/shard_map/all_to_all | solution.py:124
  278.5 170.6 %copy-start.1 = (bf16[1,1,8,64,4,256]{5,4,3,2,1,0:T(4,128)(2,1)S(1)}, bf16[1,1,8,64,4,256]{5,4,3,2,1,0:T(4,128)(2,1)}, u32[]{:S(2)}) copy-start(bf16[1,1,8,64,4,256]{5,4,3,2,1,0:T(4,128)(2,1)} %param.10) | copy-start | bytes 3145732
  (12 other events, 17.7 us)
Sparse Core Ops, SparseCore 0:
  204.7 14.2 reduce-scatter.3
  221.6 16.2 reduce-scatter.7
  241.8 205.6 reduce-scatter.5
